TPU v7x, 128 devices: a whole 4x4x4 slice. The times are simulated.
128 devices in a mesh: coil: 8 (over y, x_hi), pencil: 16 (over z, x_lo, core).
Axes of the slice: x: 4 (x_hi: 2, x_lo: 2; x = x_hi * 2 + x_lo), y: 4, z: 4, core: 2. Of those that a mesh axis runs over, the one named last changes fastest.
Arguments:
- object_image: bfloat16 [32, 256, 1024], P(None, 'pencil'), may hold values from -6 to 6
- coil_maps: bfloat16 [64, 32, 256, 1024], P('coil', None, 'pencil'), may hold values from -0.75 to 0.75
- sample_mask: int32 [32, 256, 4], replicated, may hold values 0 or 1
Outputs:
- adjoint_image: float32 [32, 256, 1024], P('coil', 'pencil')
Inputs may be any that keep to these rules, and one draw needn't show every extreme that they name: `sample_mask`: 1 where the 128 readout samples of a segment are acquired.
All inputs are finite; a program needn't handle non-finite values.
Results may differ from a plain program's by a relative error of at most 0.01.
Values may be sent and summed in bfloat16 or wider, within the bound.
No kernel may reach another device: no remote copies, remote signals or barrier semaphores. Data moves between devices by JAX's collectives and lax.ppermute only.
A program may use at most 192 MiB of HBM per device.

v0:
```python
import math
import jax
import jax.numpy as jnp
from jax import lax
from jax.sharding import PartitionSpec as P


def dft_tables(length, direction):
    indices = jnp.arange(length, dtype=jnp.int32)
    phases = indices[:, None] * indices[None, :] % length
    angles = phases.astype(jnp.float32) * (2.0 * math.pi / length)
    factor = 1.0 / math.sqrt(length)
    cosine = (jnp.cos(angles) * factor).astype(jnp.bfloat16)
    sine_part = (direction * jnp.sin(angles) * factor).astype(jnp.bfloat16)
    return (cosine, sine_part)


def readout_table(length, direction):
    cosine, sine_part = dft_tables(length, direction)
    upper = jnp.concatenate([cosine, sine_part], axis=1)
    lower = jnp.concatenate([-sine_part, cosine], axis=1)
    return jnp.concatenate([upper, lower], axis=0)


def complex_product(left_side, right_side, readout, conjugate):
    left_full = left_side.astype(jnp.float32)
    right_full = right_side.astype(jnp.float32)
    left_real = left_full[..., :readout]
    left_imag = left_full[..., readout:]
    if conjugate:
        left_imag = -left_imag
    right_real = right_full[..., :readout]
    right_imag = right_full[..., readout:]
    real_part = left_real * right_real - left_imag * right_imag
    imag_part = left_real * right_imag + left_imag * right_real
    return jnp.concatenate([real_part, imag_part], axis=-1)


def transform(volume, tables, formula, readout):
    cosine, sine_part = tables
    direct = jnp.einsum(formula, cosine, volume, preferred_element_type=jnp.float32)
    crossed = jnp.einsum(formula, sine_part, volume, preferred_element_type=jnp.float32)
    turned = jnp.concatenate([-crossed[..., readout:], crossed[..., :readout]], axis=-1)
    return (direct + turned).astype(jnp.bfloat16)


def widen(mask_part, segment):
    flags = jnp.repeat(mask_part, segment, axis=2) > 0
    return jnp.concatenate([flags, flags], axis=2)


def on_device(object_image, coil_maps, sample_mask):
    readout = object_image.shape[2] // 2
    slices = object_image.shape[0]
    row_count = object_image.shape[1]
    pencils = lax.axis_size("pencil")
    depth = slices // pencils
    lines = row_count * pencils
    segment = readout // sample_mask.shape[2]
    position = lax.axis_index("pencil")
    forward_x = readout_table(readout, -1.0)
    inverse_x = readout_table(readout, 1.0)
    forward_z = dft_tables(slices, -1.0)
    inverse_z = dft_tables(slices, 1.0)
    forward_y = dft_tables(lines, -1.0)
    inverse_y = dft_tables(lines, 1.0)
    column_mask = widen(lax.dynamic_slice_in_dim(sample_mask, position * depth, depth, 0), segment)
    nothing = jnp.zeros((), jnp.bfloat16)
    coil_image = complex_product(coil_maps, object_image[None], readout, False).astype(jnp.bfloat16)
    volume = jnp.dot(coil_image, forward_x, preferred_element_type=jnp.float32).astype(jnp.bfloat16)
    volume = transform(volume, forward_z, "kz,czyx->ckyx", readout)
    spectrum = transform(
        lax.all_to_all(volume, "pencil", split_axis=1, concat_axis=2, tiled=True),
        forward_y,
        "ky,czyx->czkx",
        readout,
    )
    spectrum = jnp.where(column_mask, spectrum, nothing)
    spectrum = transform(spectrum, inverse_y, "ky,czyx->czkx", readout)
    coil_block = lax.all_to_all(spectrum, "pencil", split_axis=2, concat_axis=1, tiled=True)
    coil_block = transform(coil_block, inverse_z, "kz,czyx->ckyx", readout)
    returned = jnp.dot(coil_block, inverse_x, preferred_element_type=jnp.float32).astype(
        jnp.bfloat16
    )
    partial_sum = jnp.sum(complex_product(coil_maps, returned, readout, True), axis=0)
    summed = lax.psum(partial_sum.astype(jnp.bfloat16), "coil").astype(jnp.float32)
    share_rows = slices // lax.axis_size("coil")
    return lax.dynamic_slice_in_dim(summed, lax.axis_index("coil") * share_rows, share_rows, 0)


def solution(mesh):
    placed = (P(None, "pencil", None), P("coil", None, "pencil", None), P())
    return jax.shard_map(
        on_device, mesh=mesh, in_specs=placed, out_specs=P("coil", "pencil", None), check_vma=False
    )
```

profile of v0, /device:TPU:0, one launch (start us, length us, event | category | flops | bytes accessed | tf_op | source)
XLA Modules:
  0.0 600.3 jit_solution(16223874633150782746)
XLA Ops:
  6.5 4.4 multiply_convert_fusion.1
  10.9 4.0 fusion.42
  14.9 0.0 copy-start
  14.9 11.5 %convert_element_type.120 = f32[8,32,16,1024]{3,2,1,0:T(8,128)} convert(bf16[8,32,16,1024]{3,2,1,0:T(8,128)(2,1)} %param.4) | non-fusion elementwise | flops 4194304 | bytes 25165824 | tf_op jit(solution)/shard_map/convert_element_type | solution.py:26
  26.5 0.0 copy-done
  26.5 0.2 bitcast_convert_fusion
  26.7 0.2 slice_bitcast_fusion.1
  26.9 7.5 %subtract_convert_fusion = (bf16[8,32,16,512]{3,2,1,0:T(8,128)(2,1)S(1)}, bf16[8,32,16,512]{3,2,1,0:T(8,128)(2,1)S(1)}) fusion(f32[8,32,16,1024]{3,2,1,0:T(8,128)} %convert_element_type.120, f32[32,16,512]{2,1,0:T(8,128)S(1)} %get-tuple-element.18, f32[32,16,512]{2,1,0:T(8,128)S(1)} %get-tuple-element.17), kind=kLoop, calls=%fused_computation.27 | loop fusion | flops 16777216 | bytes 27262976 | tf_op jit(solution)/shard_map/convert.1
  34.4 11.5 %fusion.14 = bf16[8,32,16,1024]{3,2,1,0:T(8,128)(2,1)} fusion(bf16[8,32,16,512]{3,2,1,0:T(8,128)(2,1)S(1)} %get-tuple-element.8, bf16[8,32,16,512]{3,2,1,0:T(8,128)(2,1)S(1)} %get-tuple-element.7, bf16[512,512]{1,0:T(8,128)(2,1)S(1)} %get-tuple-element.20, bf16[512,512]{1,0:T(8,128)(2,1)S(1)} %fusion.42, bf16[512,512]{1,0:T(8,128)(2,1)S(1)} %get-tuple-element.19), kind=kOutput, calls=%fused_computation.31 | convolution fusion | flops 8619294720 | bytes 18350080 | tf_op jit(solution)/shard_map/dot_general | solution.py:70
  45.9 15.0 %convolution_bitcast_fusion.1 = f32[8,32,16,1024]{3,1,2,0:T(8,128)S(1)} fusion(bf16[8,32,16,1024]{3,2,1,0:T(8,128)(2,1)} %fusion.14), kind=kOutput, calls=%fused_computation.10 | convolution fusion | flops 268451840 | bytes 25165824 | tf_op jit(solution)/shard_map/kz,czyx->ckyx/dot_general | solution.py:42
  61.0 6.8 %slice_negate_fusion.3 = (f32[8,32,16,512]{3,1,2,0:T(8,128)}, f32[8,32,16,512]{3,1,2,0:T(8,128)}) fusion(f32[8,32,16,1024]{3,1,2,0:T(8,128)S(1)} %convolution_bitcast_fusion.1), kind=kLoop, calls=%fused_computation.16 | loop fusion | flops 2097152 | bytes 33554432 | tf_op jit(solution)/shard_map/neg | solution.py:43
  67.8 26.7 %fusion = bf16[8,32,16,1024]{3,1,2,0:T(8,128)(2,1)} fusion(f32[8,32,16,512]{3,1,2,0:T(8,128)} %get-tuple-element.16, f32[8,32,16,512]{3,1,2,0:T(8,128)} %get-tuple-element.15, bf16[8,32,16,1024]{3,2,1,0:T(8,128)(2,1)} %fusion.14), kind=kOutput, calls=%fused_computation.1 | convolution fusion | flops 281034752 | bytes 33554432 | tf_op jit(solution)/shard_map/kz,czyx->ckyx/dot_general | solution.py:41
  94.5 11.3 %copy.28 = bf16[8,32,16,1024]{3,2,0,1:T(8,128)(2,1)} copy(bf16[8,32,16,1024]{3,1,2,0:T(8,128)(2,1)} %fusion) | data formatting | bytes 16777216 | tf_op jit(solution)/shard_map/convert_element_type | solution.py:44
  105.8 6.9 %all-to-all-start = ((bf16[8,32,16,1024]{3,2,0,1:T(8,128)(2,1)}), bf16[8,32,16,1024]{3,2,0,1:T(8,128)(2,1)}, u32[]{:S(2)}, u32[]{:S(2)}) async-start(bf16[8,32,16,1024]{3,2,0,1:T(8,128)(2,1)} %copy.28), calls=%async_computation | async-start | bytes 16777216 | tf_op jit(solution)/shard_map/all_to_all | solution.py:73
  112.7 0.7 dynamic-slice_compare_fusion
  113.4 0.1 broadcast_in_dim.8
  113.5 0.1 pad_add_fusion
  113.6 94.4 %all-to-all-done = bf16[8,32,16,1024]{3,2,0,1:T(8,128)(2,1)} async-done(((bf16[8,32,16,1024]{3,2,0,1:T(8,128)(2,1)}), bf16[8,32,16,1024]{3,2,0,1:T(8,128)(2,1)}, u32[]{:S(2)}, u32[]{:S(2)}) %all-to-all-start) | async-done | bytes 8388640 | tf_op jit(solution)/shard_map/all_to_all | solution.py:73
  208.0 8.5 %copy.30 = bf16[8,2,16,16,1024]{4,3,2,1,0:T(8,128)(2,1)} copy(bf16[8,2,16,16,1024]{4,3,0,1,2:T(8,128)(2,1)} %bitcast.15) | data formatting | bytes 16777216 | tf_op jit(solution)/shard_map/all_to_all | solution.py:73
  216.6 6.7 %convolution_bitcast_fusion.3 = f32[8,2,256,1024]{2,3,1,0:T(8,128)S(1)} fusion(bf16[8,2,256,1024]{3,2,1,0:T(8,128)(2,1)} %bitcast.79), kind=kOutput, calls=%fused_computation.12 | convolution fusion | flops 2148532224 | bytes 25165824 | tf_op jit(solution)/shard_map/ky,czyx->czkx/dot_general | solution.py:42
  223.3 6.3 %slice_negate_fusion.2 = (f32[8,2,256,512]{2,3,1,0:T(8,128)}, f32[8,2,256,512]{2,3,1,0:T(8,128)}) fusion(f32[8,2,256,1024]{2,3,1,0:T(8,128)S(1)} %convolution_bitcast_fusion.3), kind=kLoop, calls=%fused_computation.15 | loop fusion | flops 2097152 | bytes 33554432 | tf_op jit(solution)/shard_map/neg | solution.py:43
  229.6 13.8 %fusion.1 = bf16[8,2,256,1024]{2,3,1,0:T(8,128)(2,1)} fusion(f32[8,2,256,512]{2,3,1,0:T(8,128)} %get-tuple-element.14, f32[8,2,256,512]{2,3,1,0:T(8,128)} %get-tuple-element.13, bf16[8,2,256,1024]{3,2,1,0:T(8,128)(2,1)} %bitcast.80), kind=kOutput, calls=%fused_computation.3 | convolution fusion | flops 2161115136 | bytes 33554432 | tf_op jit(solution)/shard_map/ky,czyx->czkx/dot_general | solution.py:41
  243.4 6.7 %convolution_bitcast_fusion.2 = f32[8,2,256,1024]{2,3,1,0:T(8,128)S(1)} fusion(bf16[8,2,256,1024]{2,3,1,0:T(8,128)(2,1)} %fusion.1, pred[2,256,1024]{1,2,0:T(8,128)(4,1)S(1)} %pad_add_fusion), kind=kOutput, calls=%fused_computation.11 | convolution fusion | flops 2152726528 | bytes 25690112 | tf_op jit(solution)/shard_map/ky,czyx->czkx/dot_general | solution.py:42
  250.0 6.9 %slice_negate_fusion.1 = (f32[8,2,256,512]{2,3,1,0:T(8,128)}, f32[8,2,256,512]{2,3,1,0:T(8,128)}) fusion(f32[8,2,256,1024]{2,3,1,0:T(8,128)S(1)} %convolution_bitcast_fusion.2), kind=kLoop, calls=%fused_computation.14 | loop fusion | flops 2097152 | bytes 33554432 | tf_op jit(solution)/shard_map/neg | solution.py:43
  256.9 13.7 %fusion.2 = bf16[8,2,256,1024]{2,3,1,0:T(8,128)(2,1)} fusion(f32[8,2,256,512]{2,3,1,0:T(8,128)} %get-tuple-element.12, f32[8,2,256,512]{2,3,1,0:T(8,128)} %get-tuple-element.11, bf16[8,2,256,1024]{2,3,1,0:T(8,128)(2,1)} %fusion.1, pred[2,256,1024]{1,2,0:T(8,128)(4,1)S(1)} %pad_add_fusion), kind=kOutput, calls=%fused_computation.5 | convolution fusion | flops 2165309440 | bytes 34078720 | tf_op jit(solution)/shard_map/ky,czyx->czkx/dot_general | solution.py:41
  270.6 21.2 %copy.33 = bf16[8,2,256,1024]{3,1,0,2:T(2,128)(2,1)} copy(bf16[8,2,256,1024]{2,3,1,0:T(8,128)(2,1)} %fusion.2) | data formatting | bytes 16777216 | tf_op jit(solution)/shard_map/convert_element_type | solution.py:44
  291.8 4.8 all-to-all-start.1
  296.5 0.0 all-reduce.2.cloned.1.call-start
  296.6 4.0 fusion.43
  300.6 4.0 multiply_convert_fusion
  304.6 87.2 %all-to-all-done.1 = bf16[8,2,256,1024]{3,1,0,2:T(2,128)(2,1)} async-done(((bf16[8,2,256,1024]{3,1,0,2:T(2,128)(2,1)}), bf16[8,2,256,1024]{3,1,0,2:T(2,128)(2,1)}, u32[]{:S(2)}, u32[]{:S(2)}) %all-to-all-start.1) | async-done | bytes 8388640 | tf_op jit(solution)/shard_map/all_to_all | solution.py:80
  391.8 11.3 %copy.34 = bf16[8,2,256,1024]{3,2,1,0:T(8,128)(2,1)} copy(bf16[8,2,256,1024]{3,1,0,2:T(2,128)(2,1)} %all-to-all-done.1) | data formatting | bytes 16777216 | tf_op jit(solution)/shard_map/all_to_all | solution.py:80
  403.1 16.3 %copy.35 = bf16[8,16,2,16,1024]{4,2,1,3,0:T(2,128)(2,1)} copy(bf16[8,16,2,16,1024]{4,3,1,2,0:T(8,128)(2,1)} %bitcast.81) | data formatting | bytes 16777216 | tf_op jit(solution)/shard_map/all_to_all | solution.py:80
  419.5 13.2 %all_to_all.33 = bf16[8,32,16,1024]{3,1,2,0:T(8,128)(2,1)} reshape(bf16[8,16,2,16,1024]{4,2,1,3,0:T(2,128)(2,1)} %copy.35) | data formatting | bytes 16777216 | tf_op jit(solution)/shard_map/all_to_all | solution.py:80
  432.6 5.8 convolution_bitcast_fusion
  438.4 6.8 %slice_negate_fusion = (f32[8,32,16,512]{3,1,2,0:T(8,128)}, f32[8,32,16,512]{3,1,2,0:T(8,128)}) fusion(f32[8,32,16,1024]{3,1,2,0:T(8,128)S(1)} %convolution_bitcast_fusion), kind=kLoop, calls=%fused_computation.13 | loop fusion | flops 2097152 | bytes 33554432 | tf_op jit(solution)/shard_map/neg | solution.py:43
  445.2 12.0 %fusion.3 = bf16[8,32,16,1024]{3,1,2,0:T(8,128)(2,1)} fusion(f32[8,32,16,512]{3,1,2,0:T(8,128)} %get-tuple-element.10, f32[8,32,16,512]{3,1,2,0:T(8,128)} %get-tuple-element.9, bf16[8,32,16,1024]{3,1,2,0:T(8,128)(2,1)} %all_to_all.33), kind=kOutput, calls=%fused_computation.7 | convolution fusion | flops 281034752 | bytes 33554432 | tf_op jit(solution)/shard_map/kz,czyx->ckyx/dot_general | solution.py:41
  457.3 17.3 %convert_convert_fusion = f32[8,32,16,1024]{3,2,1,0:T(8,128)} fusion(bf16[8,32,16,1024]{3,1,2,0:T(8,128)(2,1)} %fusion.3, bf16[512,512]{1,0:T(8,128)(2,1)S(1)} %get-tuple-element.20, bf16[512,512]{1,0:T(8,128)(2,1)S(1)} %fusion.43, bf16[512,512]{1,0:T(8,128)(2,1)S(1)} %multiply_convert_fusion), kind=kOutput, calls=%fused_computation.25 | convolution fusion | flops 8606711808 | bytes 26738688 | tf_op jit(solution)/shard_map/dot_general | solution.py:82
  474.6 18.5 %multiply_subtract_fusion = (f32[8,32,16,512]{3,2,1,0:T(8,128)}, f32[8,32,16,512]{3,2,1,0:T(8,128)}) fusion(f32[8,32,16,1024]{3,2,1,0:T(8,128)} %convert_convert_fusion, f32[8,32,16,1024]{3,2,1,0:T(8,128)} %convert_element_type.120), kind=kLoop, calls=%fused_computation.24 | loop fusion | flops 14680064 | bytes 50331648 | tf_op jit(solution)/shard_map/sub | solution.py:34
  493.0 7.9 %maximum_reduce_fusion = bf16[32,16,1024]{2,1,0:T(8,128)(2,1)} fusion(f32[8,32,16,512]{3,2,1,0:T(8,128)} %get-tuple-element.6, f32[8,32,16,512]{3,2,1,0:T(8,128)} %get-tuple-element.5), kind=kLoop, calls=%fused_computation.8 | loop fusion | flops 7864320 | bytes 17825792 | tf_op jit(solution)/shard_map/reduce_sum | solution.py:85
  501.0 0.0 all-reduce.2.cloned.1.call-update
  501.0 90.6 %all-reduce.2.cloned.1.call-done = bf16[32,16,1024]{2,1,0:T(8,128)(2,1)} async-done(((bf16[32,16,1024]{2,1,0:T(8,128)(2,1)}), bf16[32,16,1024]{2,1,0:T(8,128)(2,1)}) %all-reduce.2.cloned.1.call-update) | async-done | bytes 1048592 | tf_op jit(solution)/shard_map/psum | solution.py:86
  591.6 1.6 dynamic-slice_convert_fusion
Async XLA Ops:
  14.9 11.5 %copy-start = (bf16[32,16,1024]{2,1,0:T(8,128)(2,1)S(1)}, bf16[32,16,1024]{2,1,0:T(8,128)(2,1)}, u32[]{:S(2)}) copy-start(bf16[32,16,1024]{2,1,0:T(8,128)(2,1)} %param.3) | copy-start | bytes 3145732
  105.8 102.2 %all-to-all-start = ((bf16[8,32,16,1024]{3,2,0,1:T(8,128)(2,1)}), bf16[8,32,16,1024]{3,2,0,1:T(8,128)(2,1)}, u32[]{:S(2)}, u32[]{:S(2)}) async-start(bf16[8,32,16,1024]{3,2,0,1:T(8,128)(2,1)} %copy.28), calls=%async_computation | async-start | bytes 16777216 | tf_op jit(solution)/shard_map/all_to_all | solution.py:73
  291.8 100.1 %all-to-all-start.1 = ((bf16[8,2,256,1024]{3,1,0,2:T(2,128)(2,1)}), bf16[8,2,256,1024]{3,1,0,2:T(2,128)(2,1)}, u32[]{:S(2)}, u32[]{:S(2)}) async-start(bf16[8,2,256,1024]{3,1,0,2:T(2,128)(2,1)} %copy.33), calls=%async_computation.1 | async-start | bytes 16777216 | tf_op jit(solution)/shard_map/all_to_all | solution.py:80
  296.5 295.1 %all-reduce.2.cloned.1.call-start = ((), (), s32[]{:S(2)}) async-start(), calls=%async_computation.2 | async-start | bytes 2097152 | tf_op jit(solution)/shard_map/psum | solution.py:86
Sparse Core Ops, SparseCore 0:
  501.1 90.4 all-reduce.1
where the time goes:
time: 608 us; the launch traced here: 600 us
  waiting for transfers between devices  272 us (45%)
  matrix products  129 us (21%)
  other arithmetic  91.2 us (15%)
  local copies, waits for them, and re-layouts  82.2 us (14%)
  between operations  13.8 us (2%)
  starting transfers between devices  11.7 us (2%)
    all_to_all x1, waiting for transfers between devices, on_device(): lax.all_to_all(volume, 'pencil', split_axis=1, concat_axis=2, tiled=True)  94.4 us
    psum x1, waiting for transfers between devices, on_device(): lax.psum(partial_sum.astype(jnp.bfloat16), 'coil').astype(jnp.float32)  90.6 us
    all_to_all x1, waiting for transfers between devices, on_device(): lax.all_to_all(spectrum, 'pencil', split_axis=2, concat_axis=1, tiled=True)  87.2 us
    dot_general x4, matrix products, transform(): jnp.einsum(formula, cosine, volume, preferred_element_type=jnp.float32)  66.2 us
    all_to_all x3, local copies, waits for them, and re-layouts, on_device(): lax.all_to_all(spectrum, 'pencil', split_axis=2, concat_axis=1, tiled=True)  40.8 us
    dot_general x4, matrix products, transform(): jnp.einsum(formula, sine_part, volume, preferred_element_type=jnp.float32)  34.2 us
    convert_element_type x2, local copies, waits for them, and re-layouts, transform(): return (direct + turned).astype(jnp.bfloat16)  32.5 us
    neg x4, other arithmetic, transform(): -crossed[..., readout:]  26.8 us
  transfers between devices with their start and end apart: 3, of which 3 were waited for; matrix products, arithmetic and copies ran while one was open for 1% of the time, Pallas kernels for 0%

commit v1 on v0

--- a/solution.py
+++ b/solution.py
@@ -83,7 +83,8 @@
         jnp.bfloat16
     )
     partial_sum = jnp.sum(complex_product(coil_maps, returned, readout, True), axis=0)
-    summed = lax.psum(partial_sum.astype(jnp.bfloat16), "coil").astype(jnp.float32)
+    files_measure = lambda mine_x: jnp.sum(lax.all_gather(mine_x, "coil"), 0)
+    summed = files_measure(partial_sum.astype(jnp.bfloat16)).astype(jnp.float32)
     share_rows = slices // lax.axis_size("coil")
     return lax.dynamic_slice_in_dim(summed, lax.axis_index("coil") * share_rows, share_rows, 0)
 

time: 608 us -> 630 us (1.036)
  waiting for transfers between devices: 272 us -> 288 us
    all_gather x0 -> x1, waiting for transfers between devices: none -> 107 us  [on_device(): files_measure = lambda mine_x: jnp.sum(lax.all_gather(mine_x, 'coil'), 0)]
    psum x1 -> x0, waiting for transfers between devices: 90.6 us -> none  [on_device(): lax.psum(partial_sum.astype(jnp.bfloat16), 'coil').astype(jnp.float32)]
where the time goes in v1:
time: 630 us; the launch traced here: 622 us
  waiting for transfers between devices  288 us (46%)
  matrix products  129 us (20%)
  other arithmetic  96.3 us (15%)
  local copies, waits for them, and re-layouts  82.2 us (13%)
  between operations  14 us (2%)
  starting transfers between devices  11.7 us (2%)
    all_gather x1, waiting for transfers between devices, on_device(): files_measure = lambda mine_x: jnp.sum(lax.all_gather(mine_x, 'coil'), 0)  107 us
    all_to_all x1, waiting for transfers between devices, on_device(): lax.all_to_all(volume, 'pencil', split_axis=1, concat_axis=2, tiled=True)  94.4 us
    all_to_all x1, waiting for transfers between devices, on_device(): lax.all_to_all(spectrum, 'pencil', split_axis=2, concat_axis=1, tiled=True)  87.2 us
    dot_general x4, matrix products, transform(): jnp.einsum(formula, cosine, volume, preferred_element_type=jnp.float32)  66.2 us
    all_to_all x3, local copies, waits for them, and re-layouts, on_device(): lax.all_to_all(spectrum, 'pencil', split_axis=2, concat_axis=1, tiled=True)  40.8 us
    dot_general x4, matrix products, transform(): jnp.einsum(formula, sine_part, volume, preferred_element_type=jnp.float32)  34.2 us
    convert_element_type x2, local copies, waits for them, and re-layouts, transform(): return (direct + turned).astype(jnp.bfloat16)  32.5 us
    neg x4, other arithmetic, transform(): -crossed[..., readout:]  26.8 us
  transfers between devices with their start and end apart: 3, of which 3 were waited for; matrix products, arithmetic and copies ran while one was open for 1% of the time, Pallas kernels for 0%

profile of v1, /device:TPU:0, one launch (start us, length us, event | category | flops | bytes accessed | tf_op | source)
XLA Modules:
  0.0 621.8 jit_solution(3658111433401568009)
XLA Ops:
  6.5 4.4 multiply_convert_fusion.1
  10.9 4.0 fusion.42
  14.9 0.0 copy-start
  14.9 11.5 %convert_element_type.132 = f32[8,32,16,1024]{3,2,1,0:T(8,128)} convert(bf16[8,32,16,1024]{3,2,1,0:T(8,128)(2,1)} %param.4) | non-fusion elementwise | flops 4194304 | bytes 25165824 | tf_op jit(solution)/shard_map/convert_element_type | solution.py:26
  26.5 0.0 copy-done
  26.5 0.2 bitcast_convert_fusion
  26.7 0.2 slice_bitcast_fusion.1
  26.9 7.5 %subtract_convert_fusion = (bf16[8,32,16,512]{3,2,1,0:T(8,128)(2,1)S(1)}, bf16[8,32,16,512]{3,2,1,0:T(8,128)(2,1)S(1)}) fusion(f32[8,32,16,1024]{3,2,1,0:T(8,128)} %convert_element_type.132, f32[32,16,512]{2,1,0:T(8,128)S(1)} %get-tuple-element.18, f32[32,16,512]{2,1,0:T(8,128)S(1)} %get-tuple-element.17), kind=kLoop, calls=%fused_computation.27 | loop fusion | flops 16777216 | bytes 27262976 | tf_op jit(solution)/shard_map/convert.2
  34.4 11.6 %fusion.14 = bf16[8,32,16,1024]{3,2,1,0:T(8,128)(2,1)} fusion(bf16[8,32,16,512]{3,2,1,0:T(8,128)(2,1)S(1)} %get-tuple-element.8, bf16[8,32,16,512]{3,2,1,0:T(8,128)(2,1)S(1)} %get-tuple-element.7, bf16[512,512]{1,0:T(8,128)(2,1)S(1)} %get-tuple-element.20, bf16[512,512]{1,0:T(8,128)(2,1)S(1)} %fusion.42, bf16[512,512]{1,0:T(8,128)(2,1)S(1)} %get-tuple-element.19), kind=kOutput, calls=%fused_computation.31 | convolution fusion | flops 8619294720 | bytes 18350080 | tf_op jit(solution)/shard_map/dot_general | solution.py:70
  46.0 15.0 %convolution_bitcast_fusion.1 = f32[8,32,16,1024]{3,1,2,0:T(8,128)S(1)} fusion(bf16[8,32,16,1024]{3,2,1,0:T(8,128)(2,1)} %fusion.14), kind=kOutput, calls=%fused_computation.10 | convolution fusion | flops 268451840 | bytes 25165824 | tf_op jit(solution)/shard_map/kz,czyx->ckyx/dot_general | solution.py:42
  61.1 6.8 %slice_negate_fusion.3 = (f32[8,32,16,512]{3,1,2,0:T(8,128)}, f32[8,32,16,512]{3,1,2,0:T(8,128)}) fusion(f32[8,32,16,1024]{3,1,2,0:T(8,128)S(1)} %convolution_bitcast_fusion.1), kind=kLoop, calls=%fused_computation.16 | loop fusion | flops 2097152 | bytes 33554432 | tf_op jit(solution)/shard_map/neg | solution.py:43
  67.8 26.7 %fusion = bf16[8,32,16,1024]{3,1,2,0:T(8,128)(2,1)} fusion(f32[8,32,16,512]{3,1,2,0:T(8,128)} %get-tuple-element.16, f32[8,32,16,512]{3,1,2,0:T(8,128)} %get-tuple-element.15, bf16[8,32,16,1024]{3,2,1,0:T(8,128)(2,1)} %fusion.14), kind=kOutput, calls=%fused_computation.1 | convolution fusion | flops 281034752 | bytes 33554432 | tf_op jit(solution)/shard_map/kz,czyx->ckyx/dot_general | solution.py:41
  94.5 11.3 %copy.28 = bf16[8,32,16,1024]{3,2,0,1:T(8,128)(2,1)} copy(bf16[8,32,16,1024]{3,1,2,0:T(8,128)(2,1)} %fusion) | data formatting | bytes 16777216 | tf_op jit(solution)/shard_map/convert_element_type | solution.py:44
  105.8 6.9 %all-to-all-start = ((bf16[8,32,16,1024]{3,2,0,1:T(8,128)(2,1)}), bf16[8,32,16,1024]{3,2,0,1:T(8,128)(2,1)}, u32[]{:S(2)}, u32[]{:S(2)}) async-start(bf16[8,32,16,1024]{3,2,0,1:T(8,128)(2,1)} %copy.28), calls=%async_computation | async-start | bytes 16777216 | tf_op jit(solution)/shard_map/all_to_all | solution.py:73
  112.7 0.7 dynamic-slice_compare_fusion
  113.5 0.1 broadcast_in_dim.8
  113.5 0.1 pad_add_fusion
  113.7 94.4 %all-to-all-done = bf16[8,32,16,1024]{3,2,0,1:T(8,128)(2,1)} async-done(((bf16[8,32,16,1024]{3,2,0,1:T(8,128)(2,1)}), bf16[8,32,16,1024]{3,2,0,1:T(8,128)(2,1)}, u32[]{:S(2)}, u32[]{:S(2)}) %all-to-all-start) | async-done | bytes 8388640 | tf_op jit(solution)/shard_map/all_to_all | solution.py:73
  208.1 8.5 %copy.30 = bf16[8,2,16,16,1024]{4,3,2,1,0:T(8,128)(2,1)} copy(bf16[8,2,16,16,1024]{4,3,0,1,2:T(8,128)(2,1)} %bitcast.15) | data formatting | bytes 16777216 | tf_op jit(solution)/shard_map/all_to_all | solution.py:73
  216.6 6.7 %convolution_bitcast_fusion.3 = f32[8,2,256,1024]{2,3,1,0:T(8,128)S(1)} fusion(bf16[8,2,256,1024]{3,2,1,0:T(8,128)(2,1)} %bitcast.80), kind=kOutput, calls=%fused_computation.12 | convolution fusion | flops 2148532224 | bytes 25165824 | tf_op jit(solution)/shard_map/ky,czyx->czkx/dot_general | solution.py:42
  223.3 6.3 %slice_negate_fusion.2 = (f32[8,2,256,512]{2,3,1,0:T(8,128)}, f32[8,2,256,512]{2,3,1,0:T(8,128)}) fusion(f32[8,2,256,1024]{2,3,1,0:T(8,128)S(1)} %convolution_bitcast_fusion.3), kind=kLoop, calls=%fused_computation.15 | loop fusion | flops 2097152 | bytes 33554432 | tf_op jit(solution)/shard_map/neg | solution.py:43
  229.6 13.8 %fusion.1 = bf16[8,2,256,1024]{2,3,1,0:T(8,128)(2,1)} fusion(f32[8,2,256,512]{2,3,1,0:T(8,128)} %get-tuple-element.14, f32[8,2,256,512]{2,3,1,0:T(8,128)} %get-tuple-element.13, bf16[8,2,256,1024]{3,2,1,0:T(8,128)(2,1)} %bitcast.81), kind=kOutput, calls=%fused_computation.3 | convolution fusion | flops 2161115136 | bytes 33554432 | tf_op jit(solution)/shard_map/ky,czyx->czkx/dot_general | solution.py:41
  243.4 6.7 %convolution_bitcast_fusion.2 = f32[8,2,256,1024]{2,3,1,0:T(8,128)S(1)} fusion(bf16[8,2,256,1024]{2,3,1,0:T(8,128)(2,1)} %fusion.1, pred[2,256,1024]{1,2,0:T(8,128)(4,1)S(1)} %pad_add_fusion), kind=kOutput, calls=%fused_computation.11 | convolution fusion | flops 2152726528 | bytes 25690112 | tf_op jit(solution)/shard_map/ky,czyx->czkx/dot_general | solution.py:42
  250.1 6.9 %slice_negate_fusion.1 = (f32[8,2,256,512]{2,3,1,0:T(8,128)}, f32[8,2,256,512]{2,3,1,0:T(8,128)}) fusion(f32[8,2,256,1024]{2,3,1,0:T(8,128)S(1)} %convolution_bitcast_fusion.2), kind=kLoop, calls=%fused_computation.14 | loop fusion | flops 2097152 | bytes 33554432 | tf_op jit(solution)/shard_map/neg | solution.py:43
  256.9 13.7 %fusion.2 = bf16[8,2,256,1024]{2,3,1,0:T(8,128)(2,1)} fusion(f32[8,2,256,512]{2,3,1,0:T(8,128)} %get-tuple-element.12, f32[8,2,256,512]{2,3,1,0:T(8,128)} %get-tuple-element.11, bf16[8,2,256,1024]{2,3,1,0:T(8,128)(2,1)} %fusion.1, pred[2,256,1024]{1,2,0:T(8,128)(4,1)S(1)} %pad_add_fusion), kind=kOutput, calls=%fused_computation.5 | convolution fusion | flops 2165309440 | bytes 34078720 | tf_op jit(solution)/shard_map/ky,czyx->czkx/dot_general | solution.py:41
  270.6 21.2 %copy.33 = bf16[8,2,256,1024]{3,1,0,2:T(2,128)(2,1)} copy(bf16[8,2,256,1024]{2,3,1,0:T(8,128)(2,1)} %fusion.2) | data formatting | bytes 16777216 | tf_op jit(solution)/shard_map/convert_element_type | solution.py:44
  291.8 4.8 all-to-all-start.1
  296.6 0.0 all-gather.3.cloned.1.call-start
  296.6 4.0 fusion.43
  300.6 4.0 multiply_convert_fusion
  304.6 87.2 %all-to-all-done.1 = bf16[8,2,256,1024]{3,1,0,2:T(2,128)(2,1)} async-done(((bf16[8,2,256,1024]{3,1,0,2:T(2,128)(2,1)}), bf16[8,2,256,1024]{3,1,0,2:T(2,128)(2,1)}, u32[]{:S(2)}, u32[]{:S(2)}) %all-to-all-start.1) | async-done | bytes 8388640 | tf_op jit(solution)/shard_map/all_to_all | solution.py:80
  391.9 11.3 %copy.34 = bf16[8,2,256,1024]{3,2,1,0:T(8,128)(2,1)} copy(bf16[8,2,256,1024]{3,1,0,2:T(2,128)(2,1)} %all-to-all-done.1) | data formatting | bytes 16777216 | tf_op jit(solution)/shard_map/all_to_all | solution.py:80
  403.2 16.3 %copy.35 = bf16[8,16,2,16,1024]{4,2,1,3,0:T(2,128)(2,1)} copy(bf16[8,16,2,16,1024]{4,3,1,2,0:T(8,128)(2,1)} %bitcast.82) | data formatting | bytes 16777216 | tf_op jit(solution)/shard_map/all_to_all | solution.py:80
  419.5 13.2 %all_to_all.33 = bf16[8,32,16,1024]{3,1,2,0:T(8,128)(2,1)} reshape(bf16[8,16,2,16,1024]{4,2,1,3,0:T(2,128)(2,1)} %copy.35) | data formatting | bytes 16777216 | tf_op jit(solution)/shard_map/all_to_all | solution.py:80
  432.7 5.8 convolution_bitcast_fusion
  438.5 6.8 %slice_negate_fusion = (f32[8,32,16,512]{3,1,2,0:T(8,128)}, f32[8,32,16,512]{3,1,2,0:T(8,128)}) fusion(f32[8,32,16,1024]{3,1,2,0:T(8,128)S(1)} %convolution_bitcast_fusion), kind=kLoop, calls=%fused_computation.13 | loop fusion | flops 2097152 | bytes 33554432 | tf_op jit(solution)/shard_map/neg | solution.py:43
  445.3 12.0 %fusion.3 = bf16[8,32,16,1024]{3,1,2,0:T(8,128)(2,1)} fusion(f32[8,32,16,512]{3,1,2,0:T(8,128)} %get-tuple-element.10, f32[8,32,16,512]{3,1,2,0:T(8,128)} %get-tuple-element.9, bf16[8,32,16,1024]{3,1,2,0:T(8,128)(2,1)} %all_to_all.33), kind=kOutput, calls=%fused_computation.7 | convolution fusion | flops 281034752 | bytes 33554432 | tf_op jit(solution)/shard_map/kz,czyx->ckyx/dot_general | solution.py:41
  457.3 17.3 %convert_convert_fusion = f32[8,32,16,1024]{3,2,1,0:T(8,128)} fusion(bf16[8,32,16,1024]{3,1,2,0:T(8,128)(2,1)} %fusion.3, bf16[512,512]{1,0:T(8,128)(2,1)S(1)} %get-tuple-element.20, bf16[512,512]{1,0:T(8,128)(2,1)S(1)} %fusion.43, bf16[512,512]{1,0:T(8,128)(2,1)S(1)} %multiply_convert_fusion), kind=kOutput, calls=%fused_computation.25 | convolution fusion | flops 8606711808 | bytes 26738688 | tf_op jit(solution)/shard_map/dot_general | solution.py:82
  474.6 18.5 %multiply_subtract_fusion = (f32[8,32,16,512]{3,2,1,0:T(8,128)}, f32[8,32,16,512]{3,2,1,0:T(8,128)}) fusion(f32[8,32,16,1024]{3,2,1,0:T(8,128)} %convert_convert_fusion, f32[8,32,16,1024]{3,2,1,0:T(8,128)} %convert_element_type.132), kind=kLoop, calls=%fused_computation.24 | loop fusion | flops 14680064 | bytes 50331648 | tf_op jit(solution)/shard_map/sub | solution.py:34
  493.1 8.3 %maximum_reduce_fusion = bf16[32,16,1024]{2,1,0:T(8,128)(2,1)} fusion(f32[8,32,16,512]{3,2,1,0:T(8,128)} %get-tuple-element.6, f32[8,32,16,512]{3,2,1,0:T(8,128)} %get-tuple-element.5), kind=kLoop, calls=%fused_computation.8 | loop fusion | flops 7864320 | bytes 17825792 | tf_op jit(solution)/shard_map/reduce_sum | solution.py:85
  501.3 0.0 all-gather.3.cloned.1.call-update
  501.4 106.7 %all-gather.3.cloned.1.call-done = bf16[256,16,1024]{2,1,0:T(8,128)(2,1)} async-done(((bf16[32,16,1024]{2,1,0:T(8,128)(2,1)}), bf16[256,16,1024]{2,1,0:T(8,128)(2,1)}) %all-gather.3.cloned.1.call-update) | async-done | bytes 8388624 | tf_op jit(solution)/shard_map/all_gather | solution.py:86
  608.1 5.6 reduce_sum.22
  613.8 0.7 dynamic-slice_convert_fusion
Async XLA Ops:
  14.9 11.5 %copy-start = (bf16[32,16,1024]{2,1,0:T(8,128)(2,1)S(1)}, bf16[32,16,1024]{2,1,0:T(8,128)(2,1)}, u32[]{:S(2)}) copy-start(bf16[32,16,1024]{2,1,0:T(8,128)(2,1)} %param.3) | copy-start | bytes 3145732
  105.8 102.2 %all-to-all-start = ((bf16[8,32,16,1024]{3,2,0,1:T(8,128)(2,1)}), bf16[8,32,16,1024]{3,2,0,1:T(8,128)(2,1)}, u32[]{:S(2)}, u32[]{:S(2)}) async-start(bf16[8,32,16,1024]{3,2,0,1:T(8,128)(2,1)} %copy.28), calls=%async_computation | async-start | bytes 16777216 | tf_op jit(solution)/shard_map/all_to_all | solution.py:73
  291.8 100.1 %all-to-all-start.1 = ((bf16[8,2,256,1024]{3,1,0,2:T(2,128)(2,1)}), bf16[8,2,256,1024]{3,1,0,2:T(2,128)(2,1)}, u32[]{:S(2)}, u32[]{:S(2)}) async-start(bf16[8,2,256,1024]{3,1,0,2:T(2,128)(2,1)} %copy.33), calls=%async_computation.1 | async-start | bytes 16777216 | tf_op jit(solution)/shard_map/all_to_all | solution.py:80
  296.6 311.5 %all-gather.3.cloned.1.call-start = ((), (), s32[]{:S(2)}) async-start(), calls=%async_computation.2 | async-start | bytes 9437184 | tf_op jit(solution)/shard_map/all_gather | solution.py:86
Sparse Core Ops, SparseCore 0:
  501.5 106.5 all-gather.2
